TPU v7x, 128 devices: a whole 4x4x4 slice. The times are simulated.
128 devices in a mesh: shards: 8 (over x, core), tensor: 4 (over z), section: 4 (over y).
Axes of the slice: x: 4, y: 4, z: 4, core: 2. Of those that a mesh axis runs over, the one named last changes fastest.
Arguments:
- attn_grad: bfloat16 [16, 4, 1024, 1024], P('section', None, 'shards', 'tensor'), may hold values from -60 to 60
- mlp_in_grad: bfloat16 [16, 2, 1024, 2816], P('section', None, 'shards', 'tensor'), may hold values from -60 to 60
- mlp_out_grad: bfloat16 [16, 2816, 1024], P('section', 'tensor', 'shards'), may hold values from -60 to 60
- attn_momentum: bfloat16 [16, 4, 1024, 1024], P('section', None, 'shards', 'tensor'), may hold values from -3 to 3
- mlp_in_momentum: bfloat16 [16, 2, 1024, 2816], P('section', None, 'shards', 'tensor'), may hold values from -3 to 3
- mlp_out_momentum: bfloat16 [16, 2816, 1024], P('section', 'tensor', 'shards'), may hold values from -3 to 3
- owners: int32 [16, 7], P('section'), may hold values from 0 to 31, as said below
- embed_weight: float32 [32128, 1024], P(('shards', 'tensor', 'section')), may hold values from -6 to 6
- embed_grad: bfloat16 [32128, 1024], P(('shards', 'tensor', 'section')), may hold values from -6 to 6
- embed_moment: float32 [32128, 1024], P(('shards', 'tensor', 'section')), may hold values from -3 to 3
- embed_second: float32 [32128, 1024], P(('shards', 'tensor', 'section')), may hold values from 0.01 to 1
- norm_scale: float32 [16, 2048], P('section'), may hold values from 0.5 to 1.5
- norm_partial: float32 [16, 32, 2048], P('section', ('shards', 'tensor')), may hold values from -2 to 2
- norm_moment: float32 [16, 2048], P('section'), may hold values from -3 to 3
- norm_second: float32 [16, 2048], P('section'), may hold values from 0.01 to 0.5
- bias_table: float32 [32, 16], replicated, may hold values from -3 to 3
- bias_partial: float32 [128, 32, 16], P(('shards', 'tensor', 'section')), may hold values from -2 to 2
- bias_moment: float32 [32, 16], replicated, may hold values from -3 to 3
- bias_second: float32 [32, 16], replicated, may hold values from 0.01 to 1
Outputs:
- attn_momentum_new: bfloat16 [16, 4, 1024, 1024], P('section', None, 'shards', 'tensor')
- mlp_in_momentum_new: bfloat16 [16, 2, 1024, 2816], P('section', None, 'shards', 'tensor')
- mlp_out_momentum_new: bfloat16 [16, 2816, 1024], P('section', 'tensor', 'shards')
- attn_update: float32 [16, 4, 1024, 1024], P('section', None, 'shards', 'tensor')
- mlp_in_update: float32 [16, 2, 1024, 2816], P('section', None, 'shards', 'tensor')
- mlp_out_update: float32 [16, 2816, 1024], P('section', 'tensor', 'shards')
- owner_rms: float32 [128], P(('shards', 'tensor', 'section'))
- embed_weight_new: float32 [32128, 1024], P(('shards', 'tensor', 'section'))
- embed_moment_new: float32 [32128, 1024], P(('shards', 'tensor', 'section'))
- embed_second_new: float32 [32128, 1024], P(('shards', 'tensor', 'section'))
- norm_scale_new: float32 [16, 2048], P('section')
- norm_moment_new: float32 [16, 2048], P('section')
- norm_second_new: float32 [16, 2048], P('section')
- bias_table_new: float32 [32, 16], replicated
- bias_moment_new: float32 [32, 16], replicated
- bias_second_new: float32 [32, 16], replicated
Inputs may be any that keep to these rules, and one draw needn't show every extreme that they name: Owner o names the device of index o among the 32 devices of the layer's section, in the order of the mesh (shards first); the 28 matrices of the layers of one section have distinct owners, so a device owns at most one matrix.
All inputs are finite; a program needn't handle non-finite values.
Results may differ from a plain program's by a relative error of at most 0.018.
Values may be sent and summed in bfloat16 or wider, within the bound.
No kernel may reach another device: no remote copies, remote signals or barrier semaphores. Data moves between devices by JAX's collectives and lax.ppermute only.
A program may use at most 192 MiB of HBM per device.

v0:
```python
import math
import jax
import jax.numpy as jnp
from jax import lax
from jax.sharding import PartitionSpec as P

D = 1024
FF = 2816
NS_STEPS = 2
coef_first = 3.4445
coef_second = -4.775
coef_third = 2.0315


def orthogonalize(matrix):
    norm_value = jnp.sqrt(jnp.sum(matrix * matrix))
    current = (matrix / (norm_value + 1e-07)).astype(jnp.bfloat16)
    for sweep_index in range(NS_STEPS):
        gram_form = jnp.dot(current, current.T, preferred_element_type=jnp.float32).astype(
            jnp.bfloat16
        )
        square_form = jnp.dot(gram_form, gram_form, preferred_element_type=jnp.float32)
        polynomial = (
            coef_second * gram_form.astype(jnp.float32) + coef_third * square_form
        ).astype(jnp.bfloat16)
        current = (
            coef_first * current.astype(jnp.float32)
            + jnp.dot(polynomial, current, preferred_element_type=jnp.float32)
        ).astype(jnp.bfloat16)
    rms_value = norm_value / math.sqrt(matrix.shape[0] * matrix.shape[1])
    return (current, rms_value)


def zeroed(matrix):
    return (jnp.zeros(matrix.shape, jnp.bfloat16), jnp.zeros((), jnp.float32))


def refresh(gradient, moment):
    fresh_moment = (0.95 * moment.astype(jnp.float32) + gradient.astype(jnp.float32)).astype(
        jnp.bfloat16
    )
    advance = (gradient.astype(jnp.float32) + 0.95 * fresh_moment.astype(jnp.float32)).astype(
        jnp.bfloat16
    )
    return (fresh_moment, advance)


def adamw_update(weight, gradient, moment, second, decay_rate):
    moment_new = 0.9 * moment + 0.1 * gradient
    second_new = 0.95 * second + 0.05 * gradient * gradient
    weight_new = weight - 0.02 * (moment_new / (jnp.sqrt(second_new) + 1e-08) + decay_rate * weight)
    return (weight_new, moment_new, second_new)


def on_device(
    attn_grad,
    mlp_in_grad,
    mlp_out_grad,
    attn_momentum,
    mlp_in_momentum,
    mlp_out_momentum,
    owners,
    embed_weight,
    embed_grad,
    embed_moment,
    embed_second,
    norm_scale,
    norm_partial,
    norm_moment,
    norm_second,
    bias_table,
    bias_partial,
    bias_moment,
    bias_second,
):
    shards_count = lax.axis_size("shards")
    tensor_count = lax.axis_size("tensor")
    group_count = shards_count * tensor_count
    my_index = lax.axis_index(("shards", "tensor"))
    layers_here = owners.shape[0]
    rows_block = attn_grad.shape[2]
    cols_block = attn_grad.shape[3]
    ff_block = mlp_in_grad.shape[3]
    square_width = rows_block * cols_block
    rect_width = rows_block * ff_block
    attn_fresh, attn_ahead = refresh(attn_grad, attn_momentum)
    inner_fresh, inner_ahead = refresh(mlp_in_grad, mlp_in_momentum)
    outer_fresh, outer_ahead = refresh(mlp_out_grad, mlp_out_momentum)
    rect_ahead = jnp.concatenate([inner_ahead, jnp.swapaxes(outer_ahead, 1, 2)[:, None]], axis=1)
    slots = jnp.arange(group_count, dtype=jnp.int32)
    square_owner = owners[:, :4].reshape(-1)
    rect_owner = owners[:, 4:].reshape(-1)
    square_pick = (slots[:, None] == square_owner[None, :]).astype(jnp.bfloat16)
    rect_pick = (slots[:, None] == rect_owner[None, :]).astype(jnp.bfloat16)
    square_send = jnp.dot(
        square_pick,
        attn_ahead.reshape(layers_here * 4, square_width),
        preferred_element_type=jnp.float32,
    ).astype(jnp.bfloat16)
    rect_send = jnp.dot(
        rect_pick,
        rect_ahead.reshape(layers_here * 3, rect_width),
        preferred_element_type=jnp.float32,
    ).astype(jnp.bfloat16)
    outgoing = jnp.concatenate([square_send, rect_send], axis=1)
    incoming = lax.all_to_all(
        outgoing, ("shards", "tensor"), split_axis=0, concat_axis=0, tiled=True
    )
    square_in = incoming[:, :square_width]
    rect_in = incoming[:, square_width:]
    square_whole = (
        square_in.astype(jnp.float32)
        .reshape(shards_count, tensor_count, rows_block, cols_block)
        .transpose(0, 2, 1, 3)
        .reshape(shards_count * rows_block, tensor_count * cols_block)
    )
    rect_whole = (
        rect_in.astype(jnp.float32)
        .reshape(shards_count, tensor_count, rows_block, ff_block)
        .transpose(0, 2, 1, 3)
        .reshape(shards_count * rows_block, tensor_count * ff_block)
    )
    owns_square = jnp.any(square_owner == my_index)
    owns_rect = jnp.any(rect_owner == my_index)
    square_done, square_rms = lax.cond(owns_square, orthogonalize, zeroed, square_whole)
    rect_done, rect_rms = lax.cond(owns_rect, orthogonalize, zeroed, rect_whole)
    square_back = (
        square_done.reshape(shards_count, rows_block, tensor_count, cols_block)
        .transpose(0, 2, 1, 3)
        .reshape(group_count, square_width)
    )
    rect_back = (
        rect_done.reshape(shards_count, rows_block, tensor_count, ff_block)
        .transpose(0, 2, 1, 3)
        .reshape(group_count, rect_width)
    )
    returning = jnp.concatenate([square_back, rect_back], axis=1)
    arrived = lax.all_to_all(
        returning, ("shards", "tensor"), split_axis=0, concat_axis=0, tiled=True
    )
    square_arrived = arrived[:, :square_width]
    rect_arrived = arrived[:, square_width:]
    square_rows = jnp.take(square_arrived, square_owner, axis=0).reshape(
        layers_here, 4, rows_block, cols_block
    ).astype(jnp.float32) * (0.2 * math.sqrt(D))
    rect_rows = jnp.take(rect_arrived, rect_owner, axis=0).reshape(
        layers_here, 3, rows_block, ff_block
    ).astype(jnp.float32) * (0.2 * math.sqrt(FF))
    mlp_in_update = rect_rows[:, :2]
    mlp_out_update = jnp.swapaxes(rect_rows[:, 2], 1, 2)
    owner_rms = (square_rms + rect_rms).reshape(1)
    norm_grad = lax.psum(norm_partial[:, 0].astype(jnp.bfloat16), ("shards", "tensor")).astype(
        jnp.float32
    )
    bias_grad = lax.psum(bias_partial[0], ("shards", "tensor", "section"))
    embed_results = adamw_update(
        embed_weight, embed_grad.astype(jnp.float32), embed_moment, embed_second, 0.1
    )
    norm_results = adamw_update(norm_scale, norm_grad, norm_moment, norm_second, 0.0)
    bias_results = adamw_update(bias_table, bias_grad, bias_moment, bias_second, 0.0)
    return (
        attn_fresh,
        inner_fresh,
        outer_fresh,
        square_rows,
        mlp_in_update,
        mlp_out_update,
        owner_rms,
        embed_results[0],
        embed_results[1],
        embed_results[2],
        norm_results[0],
        norm_results[1],
        norm_results[2],
        bias_results[0],
        bias_results[1],
        bias_results[2],
    )


def solution(mesh):
    placed = (
        P("section", None, "shards", "tensor"),
        P("section", None, "shards", "tensor"),
        P("section", "tensor", "shards"),
        P("section", None, "shards", "tensor"),
        P("section", None, "shards", "tensor"),
        P("section", "tensor", "shards"),
        P("section", None),
        P(("shards", "tensor", "section"), None),
        P(("shards", "tensor", "section"), None),
        P(("shards", "tensor", "section"), None),
        P(("shards", "tensor", "section"), None),
        P("section", None),
        P("section", ("shards", "tensor"), None),
        P("section", None),
        P("section", None),
        P(),
        P(("shards", "tensor", "section"), None, None),
        P(),
        P(),
    )
    return jax.shard_map(
        on_device,
        mesh=mesh,
        in_specs=placed,
        out_specs=(
            P("section", None, "shards", "tensor"),
            P("section", None, "shards", "tensor"),
            P("section", "tensor", "shards"),
            P("section", None, "shards", "tensor"),
            P("section", None, "shards", "tensor"),
            P("section", "tensor", "shards"),
            P(("shards", "tensor", "section")),
            P(("shards", "tensor", "section"), None),
            P(("shards", "tensor", "section"), None),
            P(("shards", "tensor", "section"), None),
            P("section", None),
            P("section", None),
            P("section", None),
            P(),
            P(),
            P(),
        ),
        check_vma=False,
    )
```

profile of v0, /device:TPU:0, one launch (start us, length us, event | category | flops | bytes accessed | tf_op | source)
XLA Modules:
  0.0 756.0 jit_solution(7406743752380418459)
XLA Ops:
  25.3 6.8 maximum_bitcast_fusion
  32.6 11.0 %reduce.4 = bf16[32,122880]{1,0:T(8,128)(2,1)} reduce(bf16[32,1,122880]{2,0,1:T(8,128)(2,1)} %maximum_bitcast_fusion, bf16[]{:T(256)} %broadcast.176), dimensions={1}, to_apply=%copy.71.reduce_sub_computation | reduce | bytes 15728642 | tf_op jit(solution)/shard_map/all_to_all | solution.py:106
  43.6 10.4 %reshape.205 = bf16[32,2,61440]{2,1,0:T(2,128)(2,1)} reshape(bf16[32,122880]{1,0:T(8,128)(2,1)} %reduce.4) | data formatting | bytes 15728640
  54.0 8.5 %all-to-all-start = ((bf16[32,2,61440]{2,1,0:T(2,128)(2,1)}), bf16[32,2,61440]{2,1,0:T(2,128)(2,1)}, u32[]{:S(2)}, u32[]{:S(2)}) async-start(bf16[32,2,61440]{2,1,0:T(2,128)(2,1)} %reshape.205), calls=%async_computation | async-start | bytes 15728640 | tf_op jit(solution)/shard_map/all_to_all | solution.py:106
  66.3 94.9 %all-to-all-done = bf16[32,2,61440]{2,1,0:T(2,128)(2,1)} async-done(((bf16[32,2,61440]{2,1,0:T(2,128)(2,1)}), bf16[32,2,61440]{2,1,0:T(2,128)(2,1)}, u32[]{:S(2)}, u32[]{:S(2)}) %all-to-all-start) | async-done | bytes 7864352 | tf_op jit(solution)/shard_map/all_to_all | solution.py:106
  161.2 23.7 %reshape.206 = bf16[32,1,122880]{2,1,0:T(2,128)(2,1)} reshape(bf16[32,2,61440]{2,1,0:T(2,128)(2,1)} %all-to-all-done) | data formatting | bytes 15728640
  184.9 17.1 %copy.103 = bf16[32,1,122880]{2,0,1:T(8,128)(2,1)} copy(bf16[32,1,122880]{2,1,0:T(2,128)(2,1)} %reshape.206) | data formatting | bytes 15728640
  203.9 7.6 %slice_convert_fusion = f32[32,90112]{1,0:T(8,128)} fusion(bf16[32,122880]{1,0:T(8,128)(2,1)} %bitcast.90), kind=kLoop, calls=%fused_computation.31 | loop fusion | flops 2883584 | bytes 17301504 | tf_op jit(solution)/shard_map/transpose | solution.py:120
  217.6 36.5 %conditional.2 = (bf16[1024,1024]{1,0:T(8,128)(2,1)S(1)}, f32[]{:T(128)}) conditional(s32[]{:T(128)} %convert_element_type.167, () %tuple.24, f32[8,128,4,256]{3,2,1,0:T(4,128)} %bitcast.88), branch_computations={%region_1.0_spmd, %region_2.4_spmd} | conditional | flops 12907970560 | bytes 35651640 | solution.py:125
  230.4 8.8 %add_convert_fusion.2 = bf16[1024,1024]{1,0:T(8,128)(2,1)} fusion(bf16[1024,1024]{1,0:T(8,128)(2,1)S(1)} %bitcast.108, bf16[1024,1024]{1,0:T(8,128)(2,1)} %fusion.38), kind=kOutput, calls=%fused_computation.4 | convolution fusion | flops 4304404480 | bytes 6291456 | tf_op jit(solution)/shard_map/cond/branch_1_fun/dot_general | solution.py:28
  245.2 8.8 %add_convert_fusion = bf16[1024,1024]{1,0:T(8,128)(2,1)S(1)} fusion(bf16[1024,1024]{1,0:T(8,128)(2,1)} %add_convert_fusion.2, bf16[1024,1024]{1,0:T(8,128)(2,1)} %fusion.39), kind=kOutput, calls=%fused_computation.2 | convolution fusion | flops 4304404480 | bytes 6291456 | tf_op jit(solution)/shard_map/cond/branch_1_fun/dot_general | solution.py:28
  260.1 12.1 %reshape.187 = f32[8,4,128,704]{3,2,1,0:T(8,128)} reshape(f32[32,90112]{1,0:T(8,128)} %slice_convert_fusion) | data formatting | bytes 23068672 | tf_op jit(solution)/shard_map/transpose | solution.py:120
  272.2 11.3 %conditional.3 = (bf16[1024,2816]{1,0:T(8,128)(2,1)}, f32[]{:T(128)}) conditional(s32[]{:T(128)} %convert_element_type.176, () %tuple.25, f32[8,128,4,704]{3,1,2,0:T(8,128)} %bitcast.87), branch_computations={%region_5.0_spmd, %region_6.0_spmd} | conditional | flops 27962376192 | bytes 174063744 | solution.py:126
  283.5 14.0 %reshape.204 = bf16[8,128,4,704]{3,2,1,0:T(4,128)(2,1)} reshape(bf16[1024,2816]{1,0:T(8,128)(2,1)} %get-tuple-element.25) | data formatting | bytes 11534336 | tf_op jit(solution)/shard_map/reshape | solution.py:133
  297.5 6.6 copy.104
  304.2 10.1 %reshape.182 = bf16[32,90112]{1,0:T(8,128)(2,1)} reshape(bf16[8,4,128,704]{3,2,1,0:T(8,128)(2,1)} %bitcast.93) | data formatting | bytes 11534336 | tf_op jit(solution)/shard_map/reshape | solution.py:135
  320.4 11.0 %reduce.5 = bf16[32,122880]{1,0:T(8,128)(2,1)} reduce(bf16[32,1,122880]{2,0,1:T(8,128)(2,1)} %maximum_bitcast_fusion.1, bf16[]{:T(256)} %broadcast.176), dimensions={1}, to_apply=%copy.77.reduce_sub_computation | reduce | bytes 15728642 | tf_op jit(solution)/shard_map/all_to_all | solution.py:138
  331.4 10.4 %reshape.207 = bf16[32,2,61440]{2,1,0:T(2,128)(2,1)} reshape(bf16[32,122880]{1,0:T(8,128)(2,1)} %reduce.5) | data formatting | bytes 15728640
  341.9 47.0 %all-to-all-start.1 = ((bf16[32,2,61440]{2,1,0:T(2,128)(2,1)}), bf16[32,2,61440]{2,1,0:T(2,128)(2,1)}, u32[]{:S(2)}, u32[]{:S(2)}) async-start(bf16[32,2,61440]{2,1,0:T(2,128)(2,1)} %reshape.207), calls=%async_computation.1 | async-start | bytes 15728640 | tf_op jit(solution)/shard_map/all_to_all | solution.py:138
  389.1 158.5 %psum.15 = f32[32,16]{0,1:T(8,128)S(1)} all-reduce(f32[32,16]{0,1:T(8,128)S(1)} %bitcast.112), channel_id=1, replica_groups=mesh['shards'=8,'tensor'=4,'section'=4] {'shards','tensor','section'}, use_global_device_ids=true, to_apply=%region_9.10 | all-reduce | flops 512 | bytes 4096 | tf_op jit(solution)/shard_map/psum | solution.py:155
  547.6 125.7 %psum.14 = bf16[4,2048]{1,0:T(4,128)(2,1)S(1)} all-reduce(bf16[4,2048]{1,0:T(4,128)(2,1)S(1)} %bitcast.109), channel_id=1, replica_groups=mesh['shards'=8,'tensor'=4,'section'=4] {'shards','tensor'}, use_global_device_ids=true, to_apply=%region_8.9 | all-reduce | flops 8192 | bytes 32768 | tf_op jit(solution)/shard_map/psum | solution.py:152
  677.9 23.2 %reshape.208 = bf16[32,1,122880]{2,1,0:T(2,128)(2,1)} reshape(bf16[32,2,61440]{2,1,0:T(2,128)(2,1)} %all-to-all-done.1) | data formatting | bytes 15728640
  701.0 17.1 %copy.102 = bf16[32,1,122880]{2,0,1:T(8,128)(2,1)} copy(bf16[32,1,122880]{2,1,0:T(2,128)(2,1)} %reshape.208) | data formatting | bytes 15728640
  725.4 9.0 %gather_fusion.1 = bf16[12,90112]{1,0:T(8,128)(2,1)} fusion(bf16[32,90112]{1,0:T(8,128)(2,1)} %slice.39, s32[1024]{0:T(1024)S(1)} %pad_clamp_fusion), kind=kCustom, calls=%fused_computation.1 | custom fusion | bytes 4325424 | tf_op jit(solution)/shard_map/jit(_take)/gather | solution.py:146
  (96 shorter events, 100.6 us)
Async XLA Ops:
  1.4 5.5 copy-start.16
  2.3 4.7 copy-start.8
  2.3 4.7 copy-start.9
  5.4 2.8 copy-start.4
  54.0 8.5 %copy-start.10 = (s32[4,7]{1,0:T(4,128)S(1)}, s32[4,7]{1,0:T(4,128)}, u32[]{:S(2)}) copy-start(s32[4,7]{1,0:T(4,128)} %param.29) | copy-start | bytes 340
  54.0 107.2 %all-to-all-start = ((bf16[32,2,61440]{2,1,0:T(2,128)(2,1)}), bf16[32,2,61440]{2,1,0:T(2,128)(2,1)}, u32[]{:S(2)}, u32[]{:S(2)}) async-start(bf16[32,2,61440]{2,1,0:T(2,128)(2,1)} %reshape.205), calls=%async_computation | async-start | bytes 15728640 | tf_op jit(solution)/shard_map/all_to_all | solution.py:106
  341.8 47.0 %copy-start.11 = (s32[4,7]{1,0:T(4,128)S(1)}, s32[4,7]{1,0:T(4,128)}, u32[]{:S(2)}) copy-start(s32[4,7]{1,0:T(4,128)} %param.29) | copy-start | bytes 340
  341.8 47.1 %copy-start.17 = (s32[4,3]{1,0:T(4,128)S(1)}, s32[4,3]{1,0:T(4,128)}, u32[]{:S(2)}) copy-start(s32[4,3]{1,0:T(4,128)} %copy-done.16) | copy-start | bytes 148
  341.8 47.2 %copy-start.12 = (f32[4,1,2048]{2,1,0:T(1,128)S(1)}, f32[4,1,2048]{2,1,0:T(1,128)}, u32[]{:S(2)}) copy-start(f32[4,1,2048]{2,1,0:T(1,128)} %param.35) | copy-start | bytes 98308
  341.8 47.2 %copy-start.21 = (f32[1,32,16]{1,2,0:T(8,128)S(1)}, f32[1,32,16]{1,2,0:T(8,128)}, u32[]{:S(2)}) copy-start(f32[1,32,16]{1,2,0:T(8,128)} %param.39) | copy-start | bytes 6148
  341.8 331.4 %copy-start.18 = (f32[32,16]{0,1:T(8,128)S(1)}, f32[32,16]{0,1:T(8,128)}, u32[]{:S(2)}) copy-start(f32[32,16]{0,1:T(8,128)} %param.38) | copy-start | bytes 6148
  341.8 331.4 %copy-start.19 = (f32[32,16]{0,1:T(8,128)S(1)}, f32[32,16]{0,1:T(8,128)}, u32[]{:S(2)}) copy-start(f32[32,16]{0,1:T(8,128)} %param.41) | copy-start | bytes 6148
  341.9 331.4 %copy-start.20 = (f32[32,16]{0,1:T(8,128)S(1)}, f32[32,16]{0,1:T(8,128)}, u32[]{:S(2)}) copy-start(f32[32,16]{0,1:T(8,128)} %param.40) | copy-start | bytes 6148
  341.9 332.1 %copy-start.5 = (f32[251,1024]{1,0:T(8,128)S(1)}, f32[251,1024]{1,0:T(8,128)}, u32[]{:S(2)}) copy-start(f32[251,1024]{1,0:T(8,128)} %param.30) | copy-start | bytes 3084292
  341.9 332.1 %copy-start.6 = (f32[251,1024]{1,0:T(8,128)S(1)}, f32[251,1024]{1,0:T(8,128)}, u32[]{:S(2)}) copy-start(f32[251,1024]{1,0:T(8,128)} %param.33) | copy-start | bytes 3084292
  341.9 332.0 %copy-start.7 = (f32[251,1024]{1,0:T(8,128)S(1)}, f32[251,1024]{1,0:T(8,128)}, u32[]{:S(2)}) copy-start(f32[251,1024]{1,0:T(8,128)} %param.32) | copy-start | bytes 3084292
  341.9 335.9 %all-to-all-start.1 = ((bf16[32,2,61440]{2,1,0:T(2,128)(2,1)}), bf16[32,2,61440]{2,1,0:T(2,128)(2,1)}, u32[]{:S(2)}, u32[]{:S(2)}) async-start(bf16[32,2,61440]{2,1,0:T(2,128)(2,1)} %reshape.207), calls=%async_computation.1 | async-start | bytes 15728640 | tf_op jit(solution)/shard_map/all_to_all | solution.py:138
  673.9 3.2 copy-start.13
  674.0 3.2 copy-start.14
  674.0 3.2 copy-start.15
  734.4 5.2 copy-start.22
  747.6 3.6 copy-start.1
  747.6 5.2 copy-start.2
  747.6 5.2 copy-start.23
  (1 other events, 2.8 us)
where the time goes:
time: 762 us; the launch traced here: 756 us
  blocking collectives  284 us (37%)
  local copies, waits for them, and re-layouts  204 us (27%)
  waiting for transfers between devices  94.9 us (12%)
  other arithmetic  69.7 us (9%)
  starting transfers between devices  55.5 us (7%)
  matrix products  34.6 us (5%)
  loops' own time  9.38 us (1%)
    psum x1, blocking collectives, on_device(): bias_grad = lax.psum(bias_partial[0], ('shards', 'tensor', 'section'))  159 us
    psum x1, blocking collectives, on_device(): lax.psum(norm_partial[:, 0].astype(jnp.bfloat16), ('shards', 'tensor'))  126 us
    unnamed x59, local copies, waits for them, and re-layouts  112 us
    all_to_all x1, waiting for transfers between devices, on_device(): lax.all_to_all(outgoing, ('shards', 'tensor'), split_axis=0, concat_axis=...  94.9 us
    all_to_all x1, starting transfers between devices, on_device(): lax.all_to_all(returning, ('shards', 'tensor'), split_axis=0, concat_axis...  47 us
    all_to_all x2, other arithmetic, on_device(): lax.all_to_all(outgoing, ('shards', 'tensor'), split_axis=0, concat_axis=...  17.8 us
    dot_general x2, matrix products, orthogonalize(): jnp.dot(polynomial, current, preferred_element_type=jnp.float32)  17.6 us
    all_to_all x2, other arithmetic, on_device(): lax.all_to_all(returning, ('shards', 'tensor'), split_axis=0, concat_axis...  17.2 us
  transfers between devices with their start and end apart: 2, of which 1 were waited for; matrix products, arithmetic and copies ran while one was open for 1% of the time, Pallas kernels for 0%

commit v1 on v0

--- a/solution.py
+++ b/solution.py
@@ -149,9 +149,9 @@
     mlp_in_update = rect_rows[:, :2]
     mlp_out_update = jnp.swapaxes(rect_rows[:, 2], 1, 2)
     owner_rms = (square_rms + rect_rms).reshape(1)
-    norm_grad = lax.psum(norm_partial[:, 0].astype(jnp.bfloat16), ("shards", "tensor")).astype(
-        jnp.float32
-    )
+    norm_grad = jnp.sum(
+        lax.all_gather(norm_partial[:, 0].astype(jnp.bfloat16), ("shards", "tensor")), axis=0
+    ).astype(jnp.float32)
     bias_grad = lax.psum(bias_partial[0], ("shards", "tensor", "section"))
     embed_results = adamw_update(
         embed_weight, embed_grad.astype(jnp.float32), embed_moment, embed_second, 0.1

time: 762 us -> 684 us (0.90)
  blocking collectives: 284 us -> 202 us
    all_gather x0 -> x1, blocking collectives: none -> 136 us  [on_device(): lax.all_gather(norm_partial[:, 0].astype(jnp.bfloat16), ('shards', 'tenso...]
    psum x1 -> x0, blocking collectives: 126 us -> none  [on_device(): lax.psum(norm_partial[:, 0].astype(jnp.bfloat16), ('shards', 'tensor'))]
    psum x1, blocking collectives: 159 us -> 65.6 us  [on_device(): bias_grad = lax.psum(bias_partial[0], ('shards', 'tensor', 'section'))]
    unnamed x59 -> x56, local copies, waits for them, and re-layouts: 112 us -> 113 us
  transfers between devices with their start and end apart: 2 -> 2, of which waited for: 1 -> 1; matrix products, arithmetic and copies ran while one was open for 1% -> 2% of each run, Pallas kernels for 0% -> 0%
where the time goes in v1:
time: 684 us; the launch traced here: 677 us
  local copies, waits for them, and re-layouts  204 us (30%)
  blocking collectives  202 us (30%)
  waiting for transfers between devices  94.9 us (14%)
  other arithmetic  73.5 us (11%)
  starting transfers between devices  54.9 us (8%)
  matrix products  34.6 us (5%)
  loops' own time  9.34 us (1%)
    all_gather x1, blocking collectives, on_device(): lax.all_gather(norm_partial[:, 0].astype(jnp.bfloat16), ('shards', 'tenso...  136 us
    unnamed x56, local copies, waits for them, and re-layouts  113 us
    all_to_all x1, waiting for transfers between devices, on_device(): lax.all_to_all(outgoing, ('shards', 'tensor'), split_axis=0, concat_axis=...  94.9 us
    psum x1, blocking collectives, on_device(): bias_grad = lax.psum(bias_partial[0], ('shards', 'tensor', 'section'))  65.6 us
    all_to_all x1, starting transfers between devices, on_device(): lax.all_to_all(returning, ('shards', 'tensor'), split_axis=0, concat_axis...  46.3 us
    all_to_all x2, other arithmetic, on_device(): lax.all_to_all(outgoing, ('shards', 'tensor'), split_axis=0, concat_axis=...  17.8 us
    dot_general x2, matrix products, orthogonalize(): jnp.dot(polynomial, current, preferred_element_type=jnp.float32)  17.6 us
    all_to_all x2, other arithmetic, on_device(): lax.all_to_all(returning, ('shards', 'tensor'), split_axis=0, concat_axis...  17.1 us
  transfers between devices with their start and end apart: 2, of which 1 were waited for; matrix products, arithmetic and copies ran while one was open for 2% of the time, Pallas kernels for 0%

profile of v1, /device:TPU:0, one launch (start us, length us, event | category | flops | bytes accessed | tf_op | source)
XLA Modules:
  0.0 677.2 jit_solution(14850803662192914981)
XLA Ops:
  25.3 6.9 %maximum_bitcast_fusion = bf16[32,1,122880]{2,0,1:T(8,128)(2,1)} fusion(bf16[32,90112]{1,0:T(8,128)(2,1)} %convolution_convert_fusion, bf16[32,32768]{1,0:T(8,128)(2,1)} %convolution_convert_fusion.1), kind=kLoop, calls=%fused_computation.26 | loop fusion | flops 15728640 | bytes 15728640 | tf_op jit(solution)/shard_map/all_to_all | solution.py:106
  32.7 11.0 %reduce.6 = bf16[32,122880]{1,0:T(8,128)(2,1)} reduce(bf16[32,1,122880]{2,0,1:T(8,128)(2,1)} %maximum_bitcast_fusion, bf16[]{:T(256)} %broadcast.177), dimensions={1}, to_apply=%copy.68.reduce_sub_computation | reduce | bytes 15728642 | tf_op jit(solution)/shard_map/all_to_all | solution.py:106
  43.6 10.4 %reshape.217 = bf16[32,2,61440]{2,1,0:T(2,128)(2,1)} reshape(bf16[32,122880]{1,0:T(8,128)(2,1)} %reduce.6) | data formatting | bytes 15728640
  54.0 8.6 %all-to-all-start = ((bf16[32,2,61440]{2,1,0:T(2,128)(2,1)}), bf16[32,2,61440]{2,1,0:T(2,128)(2,1)}, u32[]{:S(2)}, u32[]{:S(2)}) async-start(bf16[32,2,61440]{2,1,0:T(2,128)(2,1)} %reshape.217), calls=%async_computation | async-start | bytes 15728640 | tf_op jit(solution)/shard_map/all_to_all | solution.py:106
  66.4 94.9 %all-to-all-done = bf16[32,2,61440]{2,1,0:T(2,128)(2,1)} async-done(((bf16[32,2,61440]{2,1,0:T(2,128)(2,1)}), bf16[32,2,61440]{2,1,0:T(2,128)(2,1)}, u32[]{:S(2)}, u32[]{:S(2)}) %all-to-all-start) | async-done | bytes 7864352 | tf_op jit(solution)/shard_map/all_to_all | solution.py:106
  161.3 23.7 %reshape.218 = bf16[32,1,122880]{2,1,0:T(2,128)(2,1)} reshape(bf16[32,2,61440]{2,1,0:T(2,128)(2,1)} %all-to-all-done) | data formatting | bytes 15728640
  185.1 17.1 %copy.97 = bf16[32,1,122880]{2,0,1:T(8,128)(2,1)} copy(bf16[32,1,122880]{2,1,0:T(2,128)(2,1)} %reshape.218) | data formatting | bytes 15728640
  204.1 7.6 %slice_convert_fusion = f32[32,90112]{1,0:T(8,128)} fusion(bf16[32,122880]{1,0:T(8,128)(2,1)} %bitcast.87), kind=kLoop, calls=%fused_computation.31 | loop fusion | flops 2883584 | bytes 17301504 | tf_op jit(solution)/shard_map/transpose | solution.py:120
  217.8 36.5 %conditional.2 = (bf16[1024,1024]{1,0:T(8,128)(2,1)S(1)}, f32[]{:T(128)}) conditional(s32[]{:T(128)} %convert_element_type.176, () %tuple.24, f32[8,128,4,256]{3,2,1,0:T(4,128)} %bitcast.85), branch_computations={%region_1.0_spmd, %region_2.4_spmd} | conditional | flops 12907970560 | bytes 35651640 | solution.py:125
  230.6 8.8 %add_convert_fusion.2 = bf16[1024,1024]{1,0:T(8,128)(2,1)} fusion(bf16[1024,1024]{1,0:T(8,128)(2,1)S(1)} %bitcast.105, bf16[1024,1024]{1,0:T(8,128)(2,1)} %fusion.37), kind=kOutput, calls=%fused_computation.4 | convolution fusion | flops 4304404480 | bytes 6291456 | tf_op jit(solution)/shard_map/cond/branch_1_fun/dot_general | solution.py:28
  245.3 8.8 %add_convert_fusion = bf16[1024,1024]{1,0:T(8,128)(2,1)S(1)} fusion(bf16[1024,1024]{1,0:T(8,128)(2,1)} %add_convert_fusion.2, bf16[1024,1024]{1,0:T(8,128)(2,1)} %fusion.38), kind=kOutput, calls=%fused_computation.2 | convolution fusion | flops 4304404480 | bytes 6291456 | tf_op jit(solution)/shard_map/cond/branch_1_fun/dot_general | solution.py:28
  260.3 12.1 %reshape.197 = f32[8,4,128,704]{3,2,1,0:T(8,128)} reshape(f32[32,90112]{1,0:T(8,128)} %slice_convert_fusion) | data formatting | bytes 23068672 | tf_op jit(solution)/shard_map/transpose | solution.py:120
  272.3 11.3 %conditional.3 = (bf16[1024,2816]{1,0:T(8,128)(2,1)}, f32[]{:T(128)}) conditional(s32[]{:T(128)} %convert_element_type.185, () %tuple.25, f32[8,128,4,704]{3,1,2,0:T(8,128)} %bitcast.84), branch_computations={%region_5.0_spmd, %region_6.0_spmd} | conditional | flops 27962376192 | bytes 174063744 | solution.py:126
  283.6 14.0 %reshape.215 = bf16[8,128,4,704]{3,2,1,0:T(4,128)(2,1)} reshape(bf16[1024,2816]{1,0:T(8,128)(2,1)} %get-tuple-element.25) | data formatting | bytes 11534336 | tf_op jit(solution)/shard_map/reshape | solution.py:133
  297.6 6.6 copy.98
  304.3 10.1 %reshape.192 = bf16[32,90112]{1,0:T(8,128)(2,1)} reshape(bf16[8,4,128,704]{3,2,1,0:T(8,128)(2,1)} %bitcast.90) | data formatting | bytes 11534336 | tf_op jit(solution)/shard_map/reshape | solution.py:135
  320.5 11.0 %reduce.7 = bf16[32,122880]{1,0:T(8,128)(2,1)} reduce(bf16[32,1,122880]{2,0,1:T(8,128)(2,1)} %maximum_bitcast_fusion.1, bf16[]{:T(256)} %broadcast.177), dimensions={1}, to_apply=%copy.74.reduce_sub_computation | reduce | bytes 15728642 | tf_op jit(solution)/shard_map/all_to_all | solution.py:138
  331.5 10.4 %reshape.219 = bf16[32,2,61440]{2,1,0:T(2,128)(2,1)} reshape(bf16[32,122880]{1,0:T(8,128)(2,1)} %reduce.7) | data formatting | bytes 15728640
  341.9 46.3 %all-to-all-start.1 = ((bf16[32,2,61440]{2,1,0:T(2,128)(2,1)}), bf16[32,2,61440]{2,1,0:T(2,128)(2,1)}, u32[]{:S(2)}, u32[]{:S(2)}) async-start(bf16[32,2,61440]{2,1,0:T(2,128)(2,1)} %reshape.219), calls=%async_computation.1 | async-start | bytes 15728640 | tf_op jit(solution)/shard_map/all_to_all | solution.py:138
  388.5 136.2 %all-gather = bf16[128,1,2048]{2,1,0:T(2,128)(2,1)S(1)} all-gather(bf16[4,1,2048]{2,1,0:T(2,128)(2,1)S(1)} %convert_element_type.189), channel_id=2, replica_groups=mesh['shards'=8,'tensor'=4,'section'=4] {'shards','tensor'}, dimensions={0}, use_global_device_ids=true | all-gather | bytes 540672 | tf_op jit(solution)/shard_map/all_gather | solution.py:153
  528.3 65.6 %psum.7 = f32[32,16]{0,1:T(8,128)S(1)} all-reduce(f32[32,16]{0,1:T(8,128)S(1)} %bitcast.108), channel_id=1, replica_groups=mesh['shards'=8,'tensor'=4,'section'=4] {'shards','tensor','section'}, use_global_device_ids=true, to_apply=%region_9.10 | all-reduce | flops 512 | bytes 4096 | tf_op jit(solution)/shard_map/psum | solution.py:155
  599.0 23.6 %reshape.220 = bf16[32,1,122880]{2,1,0:T(2,128)(2,1)} reshape(bf16[32,2,61440]{2,1,0:T(2,128)(2,1)} %all-to-all-done.1) | data formatting | bytes 15728640
  622.6 17.1 %copy.96 = bf16[32,1,122880]{2,0,1:T(8,128)(2,1)} copy(bf16[32,1,122880]{2,1,0:T(2,128)(2,1)} %reshape.220) | data formatting | bytes 15728640
  647.0 8.9 %gather_fusion.1 = bf16[12,90112]{1,0:T(8,128)(2,1)} fusion(bf16[32,90112]{1,0:T(8,128)(2,1)} %slice.39, s32[1024]{0:T(1024)S(1)} %pad_clamp_fusion), kind=kCustom, calls=%fused_computation.1 | custom fusion | bytes 4325424 | tf_op jit(solution)/shard_map/jit(_take)/gather | solution.py:146
  (97 shorter events, 104.6 us)
Async XLA Ops:
  1.4 5.5 copy-start.15
  2.3 4.7 copy-start.6
  2.3 4.7 copy-start.7
  5.4 2.8 copy-start.3
  5.4 2.8 copy-start.4
  54.0 8.6 %copy-start.9 = (s32[4,7]{1,0:T(4,128)S(1)}, s32[4,7]{1,0:T(4,128)}, u32[]{:S(2)}) copy-start(s32[4,7]{1,0:T(4,128)} %param.29) | copy-start | bytes 340
  54.0 107.3 %all-to-all-start = ((bf16[32,2,61440]{2,1,0:T(2,128)(2,1)}), bf16[32,2,61440]{2,1,0:T(2,128)(2,1)}, u32[]{:S(2)}, u32[]{:S(2)}) async-start(bf16[32,2,61440]{2,1,0:T(2,128)(2,1)} %reshape.217), calls=%async_computation | async-start | bytes 15728640 | tf_op jit(solution)/shard_map/all_to_all | solution.py:106
  341.9 46.4 %copy-start.10 = (s32[4,7]{1,0:T(4,128)S(1)}, s32[4,7]{1,0:T(4,128)}, u32[]{:S(2)}) copy-start(s32[4,7]{1,0:T(4,128)} %param.29) | copy-start | bytes 340
  341.9 46.5 %copy-start.16 = (s32[4,3]{1,0:T(4,128)S(1)}, s32[4,3]{1,0:T(4,128)}, u32[]{:S(2)}) copy-start(s32[4,3]{1,0:T(4,128)} %copy-done.15) | copy-start | bytes 148
  341.9 46.6 %copy-start.11 = (f32[4,1,2048]{2,1,0:T(1,128)S(1)}, f32[4,1,2048]{2,1,0:T(1,128)}, u32[]{:S(2)}) copy-start(f32[4,1,2048]{2,1,0:T(1,128)} %param.35) | copy-start | bytes 98308
  341.9 257.1 %all-to-all-start.1 = ((bf16[32,2,61440]{2,1,0:T(2,128)(2,1)}), bf16[32,2,61440]{2,1,0:T(2,128)(2,1)}, u32[]{:S(2)}, u32[]{:S(2)}) async-start(bf16[32,2,61440]{2,1,0:T(2,128)(2,1)} %reshape.219), calls=%async_computation.1 | async-start | bytes 15728640 | tf_op jit(solution)/shard_map/all_to_all | solution.py:138
  388.3 140.0 %copy-start.20 = (f32[1,32,16]{1,2,0:T(8,128)S(1)}, f32[1,32,16]{1,2,0:T(8,128)}, u32[]{:S(2)}) copy-start(f32[1,32,16]{1,2,0:T(8,128)} %param.39) | copy-start | bytes 6148
  388.3 205.7 %copy-start.17 = (f32[32,16]{0,1:T(8,128)S(1)}, f32[32,16]{0,1:T(8,128)}, u32[]{:S(2)}) copy-start(f32[32,16]{0,1:T(8,128)} %param.38) | copy-start | bytes 6148
  388.3 205.7 %copy-start.18 = (f32[32,16]{0,1:T(8,128)S(1)}, f32[32,16]{0,1:T(8,128)}, u32[]{:S(2)}) copy-start(f32[32,16]{0,1:T(8,128)} %param.41) | copy-start | bytes 6148
  388.3 205.7 %copy-start.19 = (f32[32,16]{0,1:T(8,128)S(1)}, f32[32,16]{0,1:T(8,128)}, u32[]{:S(2)}) copy-start(f32[32,16]{0,1:T(8,128)} %param.40) | copy-start | bytes 6148
  388.3 206.3 %copy-start.5 = (f32[251,1024]{1,0:T(8,128)S(1)}, f32[251,1024]{1,0:T(8,128)}, u32[]{:S(2)}) copy-start(f32[251,1024]{1,0:T(8,128)} %param.30) | copy-start | bytes 3084292
  388.3 206.3 %copy-start.8 = (bf16[251,1024]{1,0:T(8,128)(2,1)S(1)}, bf16[251,1024]{1,0:T(8,128)(2,1)}, u32[]{:S(2)}) copy-start(bf16[251,1024]{1,0:T(8,128)(2,1)} %param.31) | copy-start | bytes 1542148
  594.6 3.7 copy-start.12
  594.6 3.7 copy-start.13
  594.6 3.7 copy-start.14
  656.0 5.2 copy-start.21
  669.1 3.6 copy-start.1
  669.1 5.2 copy-start.2
  669.1 5.2 copy-start.22
